TPU v7x, 512 devices: a whole 4x8x8 slice. The times are simulated.
512 devices in a mesh: lat: 16 (over y_hi, x, core), lon: 32 (over z, y_lo).
Axes of the slice: x: 4, y: 8 (y_hi: 2, y_lo: 4; y = y_hi * 4 + y_lo), z: 8, core: 2. Of those that a mesh axis runs over, the one named last changes fastest.
Arguments:
- queries: bfloat16 [131072, 1024], P(('lat', 'lon')), may hold values from -6 to 6
- gain: bfloat16 [1024], replicated, may hold values from 0.099609375 to 1.8984375
- w_query: bfloat16 [1024, 1024], P('lon'), may hold values from -0.1875 to 0.1875
- w_out: bfloat16 [1024, 1024], P(None, 'lon'), may hold values from -0.75 to 0.75
- kv_cache: bfloat16 [2, 32, 256, 1024], P(None, 'lat'), may hold values from -60 to 60
- nbr_lists: int32 [512, 4], P(('lat', 'lon')), may hold values from 0 to 31, as said below
- counts: int32 [512], P(('lat', 'lon')), may hold values from 1 to 4, as said below
Outputs:
- decoded: bfloat16 [131072, 1024], P(('lat', 'lon'))
Inputs may be any that keep to these rules, and one draw needn't show every extreme that they name: `nbr_lists`: query block b lies in band b // 32; band k holds latent blocks k * 2 to (k+1) * 2 - 1. Entries of b's list lie in its band or the bands beside it; its first counts[b] entries differ, the others repeat entry 0. `counts`: query blocks of the first and last band have 4 valid slots.
All inputs are finite; a program needn't handle non-finite values.
Results may differ from a plain program's by a relative error of at most 0.007.
The roundings to bfloat16 on the way count: a program that leaves them out, or rounds other values in their place, can miss the bound.
Values may be sent and summed in bfloat16 or wider, within the bound.
No kernel may reach another device: no remote copies, remote signals or barrier semaphores. Data moves between devices by JAX's collectives and lax.ppermute only.
A program may use at most 64 MiB of HBM per device.

v0:
```python
import jax
import jax.numpy as jnp
from jax import lax
from jax.sharding import PartitionSpec as P

H = 16
HD = 64
BLOCK_TOKENS = 256


def padded(array, sides, width):
    for axis, dim in sides:
        devices, length = (lax.axis_size(axis), array.shape[dim])
        up = [(i, (i + 1) % devices) for i in range(devices - 1)]
        down = [(j, i) for i, j in up]
        last = lax.slice_in_dim(array, length - width, length, axis=dim)
        initial = lax.slice_in_dim(array, 0, width, axis=dim)
        before = lax.ppermute(last, axis, up)
        after = lax.ppermute(initial, axis, down)
        array = jnp.concatenate([before, array, after], axis=dim)
    return array


def on_device(queries, gain, w_query, w_out, kv_cache, nbr_lists, counts):
    rows = queries.astype(jnp.float32)
    rowwise_scale = lax.rsqrt(jnp.mean(rows * rows, axis=1, keepdims=True) + 1e-05)
    normed = (rows * rowwise_scale * gain.astype(jnp.float32)[None, :]).astype(jnp.bfloat16)
    row_count = queries.shape[0]
    query_count = row_count // BLOCK_TOKENS
    projected = jnp.dot(
        normed,
        lax.all_gather(w_query, "lon", axis=0, tiled=True),
        preferred_element_type=jnp.float32,
    )
    query = (projected * HD ** (-0.5)).astype(jnp.bfloat16)
    q_heads = query.reshape(query_count, BLOCK_TOKENS, H, HD)
    lat_index = lax.axis_index("lat")
    blocks_here = kv_cache.shape[1]
    window = padded(kv_cache, (("lat", 1),), blocks_here)
    key_window = window[0].reshape(3 * blocks_here, BLOCK_TOKENS, H, HD)
    value_window = window[1].reshape(3 * blocks_here, BLOCK_TOKENS, H, HD)
    local_lists = nbr_lists - (lat_index - 1) * blocks_here

    def update(state, scores, is_live, value_rows, value_form):
        best, total_sum, running = state
        peak = jnp.max(scores, axis=3)
        new_best = jnp.where(is_live[:, None, None], jnp.maximum(best, peak), best)
        rescale = jnp.exp(best - new_best)
        expo = jnp.where(is_live[:, None, None, None], jnp.exp(scores - new_best[..., None]), 0.0)
        total_sum = total_sum * rescale + jnp.sum(expo, axis=3)
        mixed = jnp.einsum(
            value_form, expo.astype(jnp.bfloat16), value_rows, preferred_element_type=jnp.float32
        )
        running = running * rescale[..., None] + mixed
        return (new_best, total_sum, running)

    start_state = (
        jnp.full((query_count, BLOCK_TOKENS, H), -1e30, jnp.float32),
        jnp.zeros((query_count, BLOCK_TOKENS, H), jnp.float32),
        jnp.zeros((query_count, BLOCK_TOKENS, H, HD), jnp.float32),
    )

    def listed_step(slot_index, state):
        picked = lax.dynamic_slice_in_dim(local_lists, slot_index, 1, 1)[:, 0]
        key_rows = jnp.take(key_window, picked, axis=0)
        value_rows = jnp.take(value_window, picked, axis=0)
        scores = jnp.einsum(
            "bqhd,bkhd->bqhk", q_heads, key_rows, preferred_element_type=jnp.float32
        )
        return update(state, scores, slot_index < counts, value_rows, "bqhk,bkhd->bqhd")

    final_state = lax.fori_loop(0, jnp.max(counts), listed_step, start_state)
    attended = (
        (final_state[2] / final_state[1][..., None]).reshape(row_count, H * HD).astype(jnp.bfloat16)
    )
    decoded = jnp.dot(
        attended,
        lax.all_gather(w_out, "lon", axis=1, tiled=True),
        preferred_element_type=jnp.float32,
    )
    return decoded.astype(jnp.bfloat16)


def solution(mesh):
    placed = (
        P(("lat", "lon"), None),
        P(),
        P("lon", None),
        P(None, "lon"),
        P(None, "lat", None, None),
        P(("lat", "lon"), None),
        P(("lat", "lon")),
    )
    return jax.shard_map(
        on_device, mesh=mesh, in_specs=placed, out_specs=P(("lat", "lon"), None), check_vma=False
    )
```

profile of v0, /device:TPU:6, one launch (start us, length us, event | category | flops | bytes accessed | tf_op | source)
XLA Modules:
  0.0 351.9 jit_solution(9030099862044191392)
XLA Ops:
  6.5 0.7 all-gather.3.cloned.1.call-update
  7.3 1.9 collective-permute-start
  9.2 3.6 %collective-permute-start.1 = (bf16[2,2,256,1024]{3,2,1,0:T(8,128)(2,1)}, bf16[2,2,256,1024]{3,2,1,0:T(8,128)(2,1)}, u32[]{:S(2)}, u32[]{:S(2)}) collective-permute-start(bf16[2,2,256,1024]{3,2,1,0:T(8,128)(2,1)} %param.15), channel_id=1, source_target_pairs={{32,0},{64,32},{96,64},{128,96},{160,128},{192,160},{224,192},{256... | collective-permute-start | bytes 6291464 | tf_op jit(solution)/shard_map/ppermute | solution.py:19
  12.9 0.7 convert_element_type.25
  13.6 1.2 fusion.35
  14.8 0.7 broadcast_subtract_fusion
  15.5 19.5 %collective-permute-done = bf16[2,2,256,1024]{3,2,1,0:T(8,128)(2,1)} collective-permute-done((bf16[2,2,256,1024]{3,2,1,0:T(8,128)(2,1)}, bf16[2,2,256,1024]{3,2,1,0:T(8,128)(2,1)}, u32[]{:S(2)}, u32[]{:S(2)}) %collective-permute-start) | collective-permute-done | bytes 2097184 | tf_op jit(solution)/shard_map/ppermute | solution.py:18
  35.0 1.8 constant_dynamic-update-slice_fusion.2
  36.9 1.8 constant_dynamic-update-slice_fusion
  38.7 2.7 fusion.41
  41.5 4.7 %copy.13 = bf16[1,6,256,1024]{2,3,1,0:T(8,128)(2,1)} copy(bf16[1,6,256,1024]{3,2,1,0:T(8,128)(2,1)} %get-tuple-element.108) | data formatting | bytes 6291456 | tf_op jit(solution)/shard_map/slice | solution.py:40
  46.1 2.8 copy.15
  48.9 131.5 %all-gather.3.cloned.1.call-done = bf16[1024,1024]{1,0:T(8,128)(2,1)} async-done(((bf16[32,1024]{1,0:T(8,128)(2,1)}), bf16[1024,1024]{1,0:T(8,128)(2,1)}) %all-gather.3.cloned.1.call-update) | async-done | bytes 2097168 | tf_op jit(solution)/shard_map/all_gather | solution.py:32
  180.5 2.5 fusion.34
  183.4 34.2 %while.15 = (s32[]{:T(128)}, f32[1,256,16]{1,2,0:T(8,128)S(1)}, f32[1,256,16]{1,2,0:T(8,128)S(1)}, f32[1,256,16,64]{1,3,2,0:T(8,128)S(1)}, s32[]{:T(128)}, /*ind...) while((s32[]{:T(128)}, f32[1,256,16]{1,2,0:T(8,128)S(1)}, ...), condition=%wide.region_4.0_spmd, body=%wide.region_1.5_spmd.sunk | while | flops 276840448 | bytes 16517893 | solution.py:72
  184.0 0.6 constant_dynamic-slice_fusion.2
  186.5 1.8 bitcast_reduce_fusion.2
  189.0 2.0 fusion.54
  191.0 0.7 fusion.53
  192.4 0.6 constant_dynamic-slice_fusion.2
  194.9 1.8 bitcast_reduce_fusion.2
  197.4 2.0 fusion.54
  199.4 0.7 fusion.53
  200.8 0.6 constant_dynamic-slice_fusion.2
  203.3 1.8 bitcast_reduce_fusion.2
  205.8 2.0 fusion.54
  207.8 0.7 fusion.53
  211.7 1.8 bitcast_reduce_fusion.2
  214.2 2.0 fusion.54
  216.2 0.7 fusion.53
  217.7 124.2 %all-gather.5.cloned.1.call-done = bf16[1024,1024]{0,1:T(8,128)(2,1)} async-done(((bf16[1024,32]{0,1:T(8,128)(2,1)}), bf16[1024,1024]{0,1:T(8,128)(2,1)}) %all-gather.5.cloned.1.call-update) | async-done | bytes 2097168 | tf_op jit(solution)/shard_map/all_gather | solution.py:78
  341.9 3.1 convolution_convert_fusion
  (26 shorter events, 1.4 us)
Async XLA Ops:
  6.5 30.2 %copy-start = (bf16[2,2,256,1024]{3,2,1,0:T(8,128)(2,1)S(1)}, bf16[2,2,256,1024]{3,2,1,0:T(8,128)(2,1)}, u32[]{:S(2)}) copy-start(bf16[2,2,256,1024]{3,2,1,0:T(8,128)(2,1)} %param.15) | copy-start | bytes 6291460
  6.5 173.9 %all-gather.3.cloned.1.call-start = ((), (), s32[]{:S(2)}) async-start(), calls=%async_computation | async-start | bytes 2162688 | tf_op jit(solution)/shard_map/all_gather | solution.py:32
  7.3 334.7 %all-gather.5.cloned.1.call-start = ((), (), s32[]{:S(2)}) async-start(), calls=%async_computation.1 | async-start | bytes 2162688 | tf_op jit(solution)/shard_map/all_gather | solution.py:78
  7.3 27.7 %collective-permute-start = (bf16[2,2,256,1024]{3,2,1,0:T(8,128)(2,1)}, bf16[2,2,256,1024]{3,2,1,0:T(8,128)(2,1)}, u32[]{:S(2)}, u32[]{:S(2)}) collective-permute-start(bf16[2,2,256,1024]{3,2,1,0:T(8,128)(2,1)} %param.15), channel_id=1, source_target_pairs={{0,32},{32,64},{64,96},{96,128},{128,160},{160,192},{192,224},{224... | collective-permute-start | bytes 6291464 | tf_op jit(solution)/shard_map/ppermute | solution.py:18
  9.2 27.7 %collective-permute-start.1 = (bf16[2,2,256,1024]{3,2,1,0:T(8,128)(2,1)}, bf16[2,2,256,1024]{3,2,1,0:T(8,128)(2,1)}, u32[]{:S(2)}, u32[]{:S(2)}) collective-permute-start(bf16[2,2,256,1024]{3,2,1,0:T(8,128)(2,1)} %param.15), channel_id=1, source_target_pairs={{32,0},{64,32},{96,64},{128,96},{160,128},{192,160},{224,192},{256... | collective-permute-start | bytes 6291464 | tf_op jit(solution)/shard_map/ppermute | solution.py:19
Sparse Core Ops, SparseCore 0:
  9.4 171.0 all-gather.2
  182.6 159.3 all-gather.4
where the time goes:
time: 353 us; the launch traced here: 352 us
  waiting for transfers between devices  276 us (78%)
  matrix products  20.8 us (6%)
  local copies, waits for them, and re-layouts  16.8 us (5%)
  loops' own time  13.6 us (4%)
  between operations  13.5 us (4%)
  other arithmetic  5.63 us (2%)
  starting transfers between devices  5.6 us (2%)
    all_gather x1, waiting for transfers between devices, on_device(): lax.all_gather(w_query, 'lon', axis=0, tiled=True)  132 us
    all_gather x1, waiting for transfers between devices, on_device(): lax.all_gather(w_out, 'lon', axis=1, tiled=True)  124 us
    ppermute x1, waiting for transfers between devices, padded(): before = lax.ppermute(last, axis, up)  19.5 us
    another operation x1, loops' own time, on_device(): final_state = lax.fori_loop(0, jnp.max(counts), listed_step, start_state)  13.6 us
    dot_general x4, matrix products, update(): jnp.einsum(value_form, expo.astype(jnp.bfloat16), value_rows, preferred_e...  7.88 us
    dot_general x4, matrix products, listed_step(): jnp.einsum('bqhd,bkhd->bqhk', q_heads, key_rows, preferred_element_type=j...  7.23 us
  transfers between devices with their start and end apart: 4, of which 3 were waited for; matrix products, arithmetic and copies ran while one was open for 11% of the time, Pallas kernels for 0%

commit v1 on v0

--- a/solution.py
+++ b/solution.py
@@ -29,7 +29,9 @@
     query_count = row_count // BLOCK_TOKENS
     projected = jnp.dot(
         normed,
-        lax.all_gather(w_query, "lon", axis=0, tiled=True),
+        jnp.concatenate(
+            lax.all_to_all(jnp.stack([w_query] * lax.axis_size("lon")), "lon", 0, 0), axis=0
+        ),
         preferred_element_type=jnp.float32,
     )
     query = (projected * HD ** (-0.5)).astype(jnp.bfloat16)

time: 353 us -> 221 us (0.63)
  waiting for transfers between devices: 276 us -> 128 us
  starting transfers between devices: 5.6 us -> 19.5 us
    all_gather x1 -> x0, waiting for transfers between devices: 132 us -> none  [on_device(): lax.all_gather(w_query, 'lon', axis=0, tiled=True)]
    all_gather x1, waiting for transfers between devices: 124 us -> 62.1 us  [on_device(): lax.all_gather(w_out, 'lon', axis=1, tiled=True)]
    all_to_all x0 -> x1, waiting for transfers between devices: none -> 43.9 us  [on_device(): lax.all_to_all(jnp.stack([w_query] * lax.axis_size('lon')), 'lon', 0, 0)]
    all_to_all x0 -> x1, starting transfers between devices: none -> 13.9 us  [on_device(): lax.all_to_all(jnp.stack([w_query] * lax.axis_size('lon')), 'lon', 0, 0)]
  transfers between devices with their start and end apart: 4 -> 4, of which waited for: 3 -> 3; matrix products, arithmetic and copies ran while one was open for 11% -> 17% of each run, Pallas kernels for 0% -> 0%
where the time goes in v1:
time: 221 us; the launch traced here: 218 us
  waiting for transfers between devices  128 us (58%)
  matrix products  20.8 us (9%)
  starting transfers between devices  19.5 us (9%)
  local copies, waits for them, and re-layouts  19.4 us (9%)
  loops' own time  14.2 us (6%)
  between operations  13.5 us (6%)
  other arithmetic  3.25 us (1%)
    all_gather x1, waiting for transfers between devices, on_device(): lax.all_gather(w_out, 'lon', axis=1, tiled=True)  62.1 us
    all_to_all x1, waiting for transfers between devices, on_device(): lax.all_to_all(jnp.stack([w_query] * lax.axis_size('lon')), 'lon', 0, 0)  43.9 us
    ppermute x1, waiting for transfers between devices, padded(): before = lax.ppermute(last, axis, up)  21.6 us
    another operation x1, loops' own time, on_device(): final_state = lax.fori_loop(0, jnp.max(counts), listed_step, start_state)  14.2 us
    all_to_all x1, starting transfers between devices, on_device(): lax.all_to_all(jnp.stack([w_query] * lax.axis_size('lon')), 'lon', 0, 0)  13.9 us
    dot_general x4, matrix products, update(): jnp.einsum(value_form, expo.astype(jnp.bfloat16), value_rows, preferred_e...  7.88 us
    dot_general x4, matrix products, listed_step(): jnp.einsum('bqhd,bkhd->bqhk', q_heads, key_rows, preferred_element_type=j...  7.25 us
    slice x2, local copies, waits for them, and re-layouts, on_device(): value_window = window[1].reshape(3 * blocks_here, BLOCK_TOKENS, H, HD)  5.54 us
  transfers between devices with their start and end apart: 4, of which 3 were waited for; matrix products, arithmetic and copies ran while one was open for 17% of the time, Pallas kernels for 0%

profile of v1, /device:TPU:6, one launch (start us, length us, event | category | flops | bytes accessed | tf_op | source)
XLA Modules:
  0.0 218.4 jit_solution(8846543718287634392)
XLA Ops:
  6.5 2.6 %stack.2 = bf16[32,32,1024]{2,1,0:T(8,128)(2,1)} broadcast(bf16[32,1024]{1,0:T(8,128)(2,1)} %param.13), dimensions={1,2} | broadcast | bytes 2162688 | tf_op jit(solution)/shard_map/stack | solution.py:33
  9.1 13.9 %all-to-all-start = ((bf16[32,32,1024]{2,1,0:T(8,128)(2,1)}), bf16[32,32,1024]{2,1,0:T(8,128)(2,1)}, u32[]{:S(2)}, u32[]{:S(2)}) async-start(bf16[32,32,1024]{2,1,0:T(8,128)(2,1)} %stack.2), calls=%async_computation | async-start | bytes 4194304 | tf_op jit(solution)/shard_map/all_to_all | solution.py:33
  23.1 1.9 collective-permute-start
  25.0 3.6 %collective-permute-start.1 = (bf16[2,2,256,1024]{3,2,1,0:T(8,128)(2,1)S(1)}, bf16[2,2,256,1024]{3,2,1,0:T(8,128)(2,1)}, u32[]{:S(2)}, u32[]{:S(2)}) collective-permute-start(bf16[2,2,256,1024]{3,2,1,0:T(8,128)(2,1)S(1)} %copy-done), channel_id=1, source_target_pairs={{32,0},{64,32},{96,64},{128,96},{160,128},{192,160},{224,192},{256... | collective-permute-start | bytes 6291464 | tf_op jit(solution)/shard_map/ppermute | solution.py:19
  28.9 21.6 %collective-permute-done = bf16[2,2,256,1024]{3,2,1,0:T(8,128)(2,1)} collective-permute-done((bf16[2,2,256,1024]{3,2,1,0:T(8,128)(2,1)S(1)}, bf16[2,2,256,1024]{3,2,1,0:T(8,128)(2,1)}, u32[]{:S(2)}, u32[]{:S(2)}) %collective-permute-start) | collective-permute-done | bytes 2097184 | tf_op jit(solution)/shard_map/ppermute | solution.py:18
  50.5 1.8 constant_dynamic-update-slice_fusion.2
  52.5 1.8 constant_dynamic-update-slice_fusion
  54.3 2.7 %fusion.41 = (bf16[1,6,256,1024]{3,2,1,0:T(8,128)(2,1)S(1)}, bf16[1,6,256,1024]{3,2,1,0:T(8,128)(2,1)}) fusion(bf16[2,6,256,1024]{3,2,1,0:T(8,128)(2,1)S(1)} %constant_dynamic-update-slice_fusion), kind=kLoop, calls=%fused_computation.51 | loop fusion | bytes 12582912 | tf_op jit(solution)/shard_map/slice | solution.py:43
  57.0 4.7 %copy.13 = bf16[1,6,256,1024]{2,3,1,0:T(8,128)(2,1)} copy(bf16[1,6,256,1024]{3,2,1,0:T(8,128)(2,1)} %get-tuple-element.108) | data formatting | bytes 6291456 | tf_op jit(solution)/shard_map/slice | solution.py:42
  61.7 2.8 %copy.15 = bf16[1,6,256,1024]{2,3,1,0:T(8,128)(2,1)} copy(bf16[1,6,256,1024]{3,2,1,0:T(8,128)(2,1)S(1)} %get-tuple-element.107) | data formatting | bytes 6291456 | tf_op jit(solution)/shard_map/slice | solution.py:43
  64.5 43.9 %all-to-all-done = bf16[32,32,1024]{2,1,0:T(8,128)(2,1)} async-done(((bf16[32,32,1024]{2,1,0:T(8,128)(2,1)}), bf16[32,32,1024]{2,1,0:T(8,128)(2,1)}, u32[]{:S(2)}, u32[]{:S(2)}) %all-to-all-start) | async-done | bytes 2097184 | tf_op jit(solution)/shard_map/all_to_all | solution.py:33
  108.3 2.5 %fusion.34 = bf16[256,1024]{1,0:T(8,128)(2,1)S(1)} fusion(bf16[1024,1024]{1,0:T(8,128)(2,1)} %bitcast.22, bf16[256,1024]{1,0:T(8,128)(2,1)} %param.11, f32[1024]{0:T(1024)S(1)} %convert_element_type.25, f32[256]{0:T(256)S(1)} %add_rsqrt_fusion), kind=kOutput, calls=%fused_computation.39 | convolution fusion | flops 538443776 | bytes 3150848 | tf_op jit(solution)/shard_map/dot_general | solution.py:30
  110.9 0.2 copy.14
  111.2 34.9 %while.15 = (s32[]{:T(128)}, f32[1,256,16]{1,2,0:T(8,128)S(1)}, f32[1,256,16]{1,2,0:T(8,128)S(1)}, f32[1,256,16,64]{1,3,2,0:T(8,128)S(1)}, s32[]{:T(128)}, /*ind...) while((s32[]{:T(128)}, f32[1,256,16]{1,2,0:T(8,128)S(1)}, ...), condition=%wide.region_4.0_spmd, body=%wide.region_1.5_spmd.sunk | while | flops 276840448 | bytes 16517893 | solution.py:74
  111.9 0.6 constant_dynamic-slice_fusion.2
  114.6 1.8 bitcast_reduce_fusion.2
  117.0 2.0 fusion.54
  119.0 0.7 fusion.53
  120.4 0.6 constant_dynamic-slice_fusion.2
  123.1 1.8 bitcast_reduce_fusion.2
  125.6 2.0 fusion.54
  127.6 0.7 fusion.53
  129.0 0.6 constant_dynamic-slice_fusion.2
  131.7 1.8 bitcast_reduce_fusion.2
  134.2 2.0 fusion.54
  136.2 0.7 fusion.53
  137.6 0.6 constant_dynamic-slice_fusion.2
  140.3 1.8 bitcast_reduce_fusion.2
  142.7 2.0 fusion.54
  144.7 0.7 fusion.53
  146.2 62.1 %all-gather.2.cloned.1.call-done = bf16[1024,1024]{0,1:T(8,128)(2,1)} async-done(((bf16[1024,32]{0,1:T(8,128)(2,1)}), bf16[1024,1024]{0,1:T(8,128)(2,1)}) %all-gather.2.cloned.1.call-update) | async-done | bytes 2097168 | tf_op jit(solution)/shard_map/all_gather | solution.py:80
  208.4 3.1 %convolution_convert_fusion = bf16[256,1024]{1,0:T(8,128)(2,1)} fusion(bf16[256,1024]{0,1:T(8,128)(2,1)S(1)} %bitcast.109, bf16[1024,1024]{0,1:T(8,128)(2,1)} %all-gather.2.cloned.1.call-done), kind=kOutput, calls=%fused_computation.38 | convolution fusion | flops 537133056 | bytes 3145728 | tf_op jit(solution)/shard_map/dot_general | solution.py:78
  (32 shorter events, 0.8 us)
Async XLA Ops:
  6.5 16.5 %copy-start = (bf16[2,2,256,1024]{3,2,1,0:T(8,128)(2,1)S(1)}, bf16[2,2,256,1024]{3,2,1,0:T(8,128)(2,1)}, u32[]{:S(2)}) copy-start(bf16[2,2,256,1024]{3,2,1,0:T(8,128)(2,1)} %param.15) | copy-start | bytes 6291460
  6.5 22.1 %copy-start.2 = (bf16[1024]{0:T(1024)(128)(2,1)S(1)}, bf16[1024]{0:T(1024)(128)(2,1)}, u32[]{:S(2)}) copy-start(bf16[1024]{0:T(1024)(128)(2,1)} %param.12) | copy-start | bytes 6148
  6.5 22.2 %copy-start.1 = (bf16[256,1024]{1,0:T(8,128)(2,1)S(1)}, bf16[256,1024]{1,0:T(8,128)(2,1)}, u32[]{:S(2)}) copy-start(bf16[256,1024]{1,0:T(8,128)(2,1)} %param.11) | copy-start | bytes 1572868
  6.5 22.4 %copy-start.3 = (s32[1,4]{1,0:T(1,128)S(1)}, s32[1,4]{1,0:T(1,128)}, u32[]{:S(2)}) copy-start(s32[1,4]{1,0:T(1,128)} %param.16) | copy-start | bytes 52
  9.1 99.2 %all-to-all-start = ((bf16[32,32,1024]{2,1,0:T(8,128)(2,1)}), bf16[32,32,1024]{2,1,0:T(8,128)(2,1)}, u32[]{:S(2)}, u32[]{:S(2)}) async-start(bf16[32,32,1024]{2,1,0:T(8,128)(2,1)} %stack.2), calls=%async_computation | async-start | bytes 4194304 | tf_op jit(solution)/shard_map/all_to_all | solution.py:33
  23.0 185.4 %all-gather.2.cloned.1.call-start = ((), (), s32[]{:S(2)}) async-start(), calls=%async_computation.1 | async-start | bytes 2162688 | tf_op jit(solution)/shard_map/all_gather | solution.py:80
  23.1 27.5 %collective-permute-start = (bf16[2,2,256,1024]{3,2,1,0:T(8,128)(2,1)S(1)}, bf16[2,2,256,1024]{3,2,1,0:T(8,128)(2,1)}, u32[]{:S(2)}, u32[]{:S(2)}) collective-permute-start(bf16[2,2,256,1024]{3,2,1,0:T(8,128)(2,1)S(1)} %copy-done), channel_id=1, source_target_pairs={{0,32},{32,64},{64,96},{96,128},{128,160},{160,192},{192,224},{224... | collective-permute-start | bytes 6291464 | tf_op jit(solution)/shard_map/ppermute | solution.py:18
  25.0 27.5 %collective-permute-start.1 = (bf16[2,2,256,1024]{3,2,1,0:T(8,128)(2,1)S(1)}, bf16[2,2,256,1024]{3,2,1,0:T(8,128)(2,1)}, u32[]{:S(2)}, u32[]{:S(2)}) collective-permute-start(bf16[2,2,256,1024]{3,2,1,0:T(8,128)(2,1)S(1)} %copy-done), channel_id=1, source_target_pairs={{32,0},{64,32},{96,64},{128,96},{160,128},{192,160},{224,192},{256... | collective-permute-start | bytes 6291464 | tf_op jit(solution)/shard_map/ppermute | solution.py:19
Sparse Core Ops, SparseCore 0:
  28.8 179.5 all-gather.1
